TPU v7x, 32 devices: a whole 2x2x4 slice. The times are simulated.
32 devices in a mesh: snode: 16 (over z, y, x), row: 2 (over core).
Axes of the slice: x: 2, y: 2, z: 4, core: 2. Of those that a mesh axis runs over, the one named last changes fastest.
Arguments:
- ancestor_sigma: bfloat16 [8192, 8192], P('row', 'snode'), may hold values from -8 to 8, as said below
- child_panels: bfloat16 [96, 4096, 128], P('snode', 'row'), may hold values from -1 to 1
- diagonal_inverse_blocks: float32 [96, 128, 128], P('snode', 'row'), may hold values from -4 to 4, as said below
- block_list: int32 [96, 32], P('snode'), may hold values from 0 to 63, as said below
- block_count: int32 [96], P('snode'), may hold values from 8 to 32, as said below
- child_width: int32 [96], P('snode'), may hold values from 64 to 128, as said below
- owner_slot: int32 [64], replicated, may hold values from 0 to 63, each once
Outputs:
- selected_panel_inverse: float32 [8192, 96, 128], P('row', 'snode')
- selected_diagonal_inverse: float32 [96, 128, 128], P('snode', 'row')
Inputs may be any that keep to these rules, and one draw needn't show every extreme that they name: `ancestor_sigma`: symmetric. `diagonal_inverse_blocks`: each child's block is symmetric. `block_list`: the 32 entries of a row are distinct and ascending. `block_count`: some child has exactly 32. `child_width`: some child has exactly 128.
All inputs are finite; a program needn't handle non-finite values.
Results may differ from a plain program's by a relative error of at most 0.0003.
Values may be sent and summed in bfloat16 or wider, within the bound.
No kernel may reach another device: no remote copies, remote signals or barrier semaphores. Data moves between devices by JAX's collectives and lax.ppermute only.
A program may use at most 192 MiB of HBM per device.

v0:
```python
import jax
import jax.numpy as jnp
from jax import lax
from jax.sharding import PartitionSpec as P

B = 128
KMAX = 32
WJ = 128
NB = 64


def slot_table(block_list, block_count, child_width, owner_slot):
    block_ids = jnp.arange(NB, dtype=jnp.int32)
    named = block_list[:, :, None] == block_ids[None, None, :]
    slot_ids = jnp.sum(jnp.where(named, owner_slot[None, None, :], 0), axis=2)
    valid_blocks = jnp.arange(KMAX, dtype=jnp.int32)[None, :] < block_count[:, None]
    placed = (slot_ids[:, :, None] == block_ids[None, None, :]) & valid_blocks[:, :, None]
    active_columns = jnp.arange(WJ, dtype=jnp.int32)[None, :] < child_width[:, None]
    return (placed, active_columns)


def expand_rows(place_table, blocks):
    children = blocks.shape[0]
    spread = jnp.einsum("ckn,ckbj->nbcj", place_table, blocks, preferred_element_type=jnp.float32)
    return spread.astype(jnp.bfloat16).reshape(place_table.shape[2] * B, children * WJ)


def body(
    ancestor_sigma,
    child_panels,
    diagonal_inverse_blocks,
    block_list,
    block_count,
    child_width,
    owner_slot,
):
    row_devices = lax.axis_size("row")
    row_positions = lax.axis_index("row")
    children = child_panels.shape[0]
    local_rows = ancestor_sigma.shape[0]
    placed, active_columns = slot_table(block_list, block_count, child_width, owner_slot)
    place_bf = placed.astype(jnp.bfloat16)
    if row_devices == 2:
        partner = lax.ppermute(child_panels, "row", [(0, 1), (1, 0)])
        first = row_positions == 0
        gathered = jnp.concatenate(
            [jnp.where(first, child_panels, partner), jnp.where(first, partner, child_panels)],
            axis=1,
        )
    else:
        gathered = lax.all_gather(child_panels, "row", axis=1, tiled=True)
    blocks = gathered.reshape(children, KMAX, B, WJ)
    blocks = jnp.where(active_columns[:, None, None, :], blocks, jnp.zeros_like(blocks))
    panel_rows = expand_rows(place_bf, blocks)
    flipped = lax.all_gather(ancestor_sigma.T, "snode", axis=0, tiled=True)
    product = lax.dot_general(
        flipped, panel_rows, (((0,), (0,)), ((), ())), preferred_element_type=jnp.float32
    )
    product_table = product.reshape(local_rows, children, WJ)
    own_blocks = local_rows // B
    own_table = lax.dynamic_slice_in_dim(place_bf, row_positions * own_blocks, own_blocks, 2)
    own_rows = expand_rows(own_table, blocks).reshape(local_rows, children, WJ)
    partial_value = jnp.einsum(
        "nca,ncb->cab", own_rows.astype(jnp.float32), product_table, precision=lax.Precision.HIGHEST
    )
    shared_rows = WJ // row_devices
    if row_devices == 2:
        reduced_total = partial_value + lax.ppermute(partial_value, "row", [(0, 1), (1, 0)])
    else:
        reduced_total = lax.psum(partial_value, "row")
    reduced_total = lax.dynamic_slice_in_dim(
        reduced_total, row_positions * shared_rows, shared_rows, 1
    )
    active_flags = active_columns.astype(jnp.float32)
    owned_active = lax.dynamic_slice_in_dim(
        active_flags, row_positions * shared_rows, shared_rows, 1
    )
    selected_diagonal_inverse = (
        (diagonal_inverse_blocks + reduced_total)
        * owned_active[:, :, None]
        * active_flags[:, None, :]
    )
    slot_live = jnp.sum(placed.astype(jnp.float32), axis=1)
    own_slots = lax.dynamic_slice_in_dim(slot_live, row_positions * own_blocks, own_blocks, 1)
    active_rows = jnp.repeat(own_slots.T, B, axis=0)
    selected_panel_inverse = -product_table * active_rows[:, :, None] * active_flags[None, :, :]
    return (selected_panel_inverse, selected_diagonal_inverse)


def solution(mesh):
    placed = (
        P("row", "snode"),
        P("snode", "row", None),
        P("snode", "row", None),
        P("snode", None),
        P("snode"),
        P("snode"),
        P(),
    )
    return jax.shard_map(
        body,
        mesh=mesh,
        in_specs=placed,
        out_specs=(P("row", "snode", None), P("snode", "row", None)),
        check_vma=False,
    )
```

profile of v0, /device:TPU:1, one launch (start us, length us, event | category | flops | bytes accessed | tf_op | source)
XLA Modules:
  0.0 898.8 jit_solution(4280391396216717396)
XLA Ops:
  7.2 0.0 copy-start
  7.2 0.0 all-gather.2.cloned.1.call-start
  7.2 0.7 all-gather.2.cloned.1.call-update
  7.9 0.1 collective-permute-start
  8.0 1.0 select_reduce_fusion
  9.1 0.7 iota_compare_fusion.2
  9.8 0.1 convert_reduce_fusion
  9.9 0.1 dynamic-slice_bitcast_fusion
  10.0 0.1 broadcast_bitcast_fusion
  10.1 0.1 copy.45
  10.2 0.7 fusion.16
  10.9 0.1 constant_dynamic-slice_fusion
  11.0 3.0 collective-permute-done
  14.0 0.0 copy-done
  14.0 2.3 broadcast_select_fusion.1
  16.3 0.4 pad_maximum_fusion
  16.7 4.0 convert_bitcast_fusion.1
  20.7 5.8 copy.24
  26.4 7.1 convert_bitcast_fusion
  33.5 18.0 %copy.22 = bf16[64,128,6,128]{1,0,3,2:T(8,128)(2,1)} copy(bf16[64,128,6,128]{3,0,1,2:T(8,128)(2,1)} %convert_bitcast_fusion) | data formatting | bytes 25165824 | tf_op jit(solution)/shard_map/convert_element_type | solution.py:25
  51.4 685.6 %all-gather.2.cloned.1.call-done = bf16[8192,4096]{0,1:T(8,128)(2,1)} async-done(((bf16[512,4096]{0,1:T(8,128)(2,1)}), bf16[8192,4096]{0,1:T(8,128)(2,1)}) %all-gather.2.cloned.1.call-update) | async-done | bytes 67108880 | tf_op jit(solution)/shard_map/all_gather | solution.py:55
  737.1 117.5 %fusion = f32[768,4096]{1,0:T(8,128)} fusion(bf16[8192,4096]{0,1:T(8,128)(2,1)} %all-gather.2.cloned.1.call-done, bf16[96,8,64,128]{3,2,1,0:T(8,128)(2,1)} %bitcast.44), kind=kOutput, calls=%fused_computation | convolution fusion | flops 51539607552 | bytes 92274688 | tf_op jit(solution)/shard_map/dot_general | solution.py:56
  854.6 12.6 %copy.23 = f32[4096,6,128]{2,0,1:T(8,128)} copy(f32[4096,6,128]{0,2,1:T(8,128)} %bitcast.39) | data formatting | bytes 25165824 | tf_op jit(solution)/shard_map/reshape | solution.py:59
  867.2 11.1 %fusion.18 = f32[6,128,128]{2,1,0:T(8,128)S(1)} fusion(bf16[4096,6,128]{2,0,1:T(8,128)(2,1)} %bitcast.43, f32[4096,6,128]{0,2,1:T(8,128)} %bitcast.40), kind=kOutput, calls=%fused_computation.35 | convolution fusion | flops 4831838208 | bytes 19267584 | tf_op jit(solution)/shard_map/nca,ncb->cab/dot_general | solution.py:63
  878.3 1.2 collective-permute-start.1
  879.4 0.0 copy-start.1
  879.4 11.7 %multiply_multiply_fusion = f32[4096,6,128]{2,0,1:T(8,128)} fusion(f32[4096,6,128]{2,0,1:T(8,128)} %copy.23, f32[6,128]{1,0:T(8,128)S(1)} %get-tuple-element.4, f32[4096,6]{0,1:T(8,128)S(1)} %bitcast.46), kind=kLoop, calls=%fused_computation.3 | loop fusion | flops 9437184 | bytes 25267200 | tf_op jit(solution)/shard_map/mul | solution.py:86
  891.1 0.0 collective-permute-done.1
  891.1 0.0 copy-done.1
  891.1 0.8 fusion.8
  (1 shorter events, 0.0 us)
Async XLA Ops:
  7.2 6.8 copy-start
  7.2 729.9 %all-gather.2.cloned.1.call-start = ((), (), s32[]{:S(2)}) async-start(), calls=%async_computation | async-start | bytes 71303168 | tf_op jit(solution)/shard_map/all_gather | solution.py:55
  7.9 6.1 collective-permute-start
  878.3 12.8 %collective-permute-start.1 = (f32[6,128,128]{2,1,0:T(8,128)S(1)}, f32[6,128,128]{2,1,0:T(8,128)S(1)}, u32[]{:S(2)}, u32[]{:S(2)}) collective-permute-start(f32[6,128,128]{2,1,0:T(8,128)S(1)} %fusion.18), channel_id=1, source_target_pairs={{0,1},{1,0},{2,3},{3,2},{4,5},{5,4},{6,7},{7,6},{8,9},{9,8},{10,11... | collective-permute-start | bytes 1179656 | tf_op jit(solution)/shard_map/ppermute | solution.py:68
  879.4 11.7 %copy-start.1 = (f32[6,64,128]{2,1,0:T(8,128)S(1)}, f32[6,64,128]{2,1,0:T(8,128)}, u32[]{:S(2)}) copy-start(f32[6,64,128]{2,1,0:T(8,128)} %param.9) | copy-start | bytes 589828
Sparse Core Ops, SparseCore 0:
  10.8 726.2 all-gather.1
where the time goes:
time: 900 us; the launch traced here: 899 us
  waiting for transfers between devices  689 us (77%)
  matrix products  140 us (16%)
  local copies, waits for them, and re-layouts  36.6 us (4%)
  other arithmetic  17.9 us (2%)
  between operations  14.1 us (2%)
    all_gather x1, waiting for transfers between devices, body(): flipped = lax.all_gather(ancestor_sigma.T, 'snode', axis=0, tiled=True)  686 us
    dot_general x1, matrix products, body(): lax.dot_general(flipped, panel_rows, (((0,), (0,)), ((), ())), preferred_...  118 us
    convert_element_type x2, local copies, waits for them, and re-layouts, expand_rows(): spread.astype(jnp.bfloat16).reshape(place_table.shape[2] * B, children * WJ)  23.7 us
  transfers between devices with their start and end apart: 3, of which 2 were waited for; matrix products, arithmetic and copies ran while one was open for 6% of the time, Pallas kernels for 0%

commit v1 on v0

--- a/solution.py
+++ b/solution.py
@@ -52,7 +52,14 @@
     blocks = gathered.reshape(children, KMAX, B, WJ)
     blocks = jnp.where(active_columns[:, None, None, :], blocks, jnp.zeros_like(blocks))
     panel_rows = expand_rows(place_bf, blocks)
-    flipped = lax.all_gather(ancestor_sigma.T, "snode", axis=0, tiled=True)
+    ways, here = (lax.axis_size("snode"), lax.axis_index("snode"))
+    flipped, reach = (ancestor_sigma.T, 1)
+    while reach < ways:
+        theirs = lax.ppermute(flipped, "snode", [(d, d ^ reach) for d in range(ways)])
+        mine_first = jnp.concatenate([flipped, theirs], axis=0)
+        theirs_first = jnp.concatenate([theirs, flipped], axis=0)
+        flipped = jnp.where(here & reach == 0, mine_first, theirs_first)
+        reach = 2 * reach
     product = lax.dot_general(
         flipped, panel_rows, (((0,), (0,)), ((), ())), preferred_element_type=jnp.float32
     )

time: 900 us -> 2270 us (2.52)
  waiting for transfers between devices: 689 us -> 2010 us
  other arithmetic: 17.9 us -> 70.5 us
    ppermute x0 -> x4, waiting for transfers between devices: none -> 2010 us  [body(): lax.ppermute(flipped, 'snode', [(d, d ^ reach) for d in range(ways)])]
    all_gather x1 -> x0, waiting for transfers between devices: 686 us -> none  [body(): flipped = lax.all_gather(ancestor_sigma.T, 'snode', axis=0, tiled=True)]
    select_n x0 -> x3, other arithmetic: none -> 66.4 us  [body(): flipped = jnp.where(here & reach == 0, mine_first, theirs_first)]
  transfers between devices with their start and end apart: 3 -> 6, of which waited for: 2 -> 6; matrix products, arithmetic and copies ran while one was open for 6% -> 2% of each run, Pallas kernels for 0% -> 0%
where the time goes in v1:
time: 2270 us
  waiting for transfers between devices  2010 us (89%)
  matrix products  138 us (6%)
  other arithmetic  70.5 us (3%)
  local copies, waits for them, and re-layouts  39.2 us (2%)
    ppermute x4, waiting for transfers between devices, body(): lax.ppermute(flipped, 'snode', [(d, d ^ reach) for d in range(ways)])  2010 us
    dot_general x1, matrix products, body(): lax.dot_general(flipped, panel_rows, (((0,), (0,)), ((), ())), preferred_...  115 us
    select_n x3, other arithmetic, body(): flipped = jnp.where(here & reach == 0, mine_first, theirs_first)  66.4 us
  transfers between devices with their start and end apart: 6, of which 6 were waited for; matrix products, arithmetic and copies ran while one was open for 2% of the time, Pallas kernels for 0%

profile of v1, /device:TPU:1, one launch (start us, length us, event | category | flops | bytes accessed | tf_op | source)
XLA Modules:
  0.0 2272.0 jit_solution(3923170294093734676)
XLA Ops:
  0.6 2.1 collective-permute-start
  2.7 90.6 %collective-permute-done = bf16[512,4096]{0,1:T(8,128)(2,1)} collective-permute-done((bf16[512,4096]{0,1:T(8,128)(2,1)}, bf16[512,4096]{0,1:T(8,128)(2,1)}, u32[]{:S(2)}, u32[]{:S(2)}) %collective-permute-start) | collective-permute-done | bytes 4194336 | tf_op jit(solution)/shard_map/ppermute | solution.py:58
  93.3 11.5 maximum_select_fusion.3
  104.9 1.2 collective-permute-start.1
  106.0 179.9 %collective-permute-done.1 = bf16[1024,4096]{0,1:T(8,128)(2,1)} collective-permute-done((bf16[1024,4096]{0,1:T(8,128)(2,1)}, bf16[1024,4096]{0,1:T(8,128)(2,1)}, u32[]{:S(2)}, u32[]{:S(2)}) %collective-permute-start.1) | collective-permute-done | bytes 8388640 | tf_op jit(solution)/shard_map/ppermute | solution.py:58
  285.9 20.7 maximum_select_fusion.2
  306.6 0.9 collective-permute-start.2
  307.5 358.9 %collective-permute-done.2 = bf16[2048,4096]{0,1:T(8,128)(2,1)} collective-permute-done((bf16[2048,4096]{0,1:T(8,128)(2,1)}, bf16[2048,4096]{0,1:T(8,128)(2,1)}, u32[]{:S(2)}, u32[]{:S(2)}) %collective-permute-start.2) | collective-permute-done | bytes 16777248 | tf_op jit(solution)/shard_map/ppermute | solution.py:58
  666.5 34.2 %maximum_select_fusion.1 = bf16[4096,4096]{0,1:T(8,128)(2,1)} fusion(bf16[2048,4096]{0,1:T(8,128)(2,1)} %collective-permute-done.2, bf16[2048,4096]{0,1:T(8,128)(2,1)} %maximum_select_fusion.2, pred[]{:T(512)S(6)} %eq.42), kind=kLoop, calls=%fused_computation.4 | loop fusion | flops 150994944 | bytes 67108864 | tf_op jit(solution)/shard_map/jit(_where)/select_n | solution.py:61
  700.7 1.7 collective-permute-start.3
  702.3 3.7 collective-permute-start.4
  706.0 0.3 select_reduce_fusion
  706.3 0.1 iota_compare_fusion.2
  706.3 0.1 convert_reduce_fusion
  706.5 0.1 dynamic-slice_bitcast_fusion
  706.6 0.1 broadcast_bitcast_fusion
  706.7 0.1 fusion.18
  706.8 4.6 collective-permute-done.4
  711.4 2.3 broadcast_select_fusion.1
  713.7 0.4 pad_maximum_fusion
  714.1 4.0 convert_bitcast_fusion.1
  718.1 5.2 copy.19
  723.3 7.1 convert_bitcast_fusion
  730.3 17.9 copy.18
  748.2 15.8 copy.35
  764.0 1378.3 %collective-permute-done.3 = bf16[4096,4096]{0,1:T(8,128)(2,1)} collective-permute-done((bf16[4096,4096]{0,1:T(8,128)(2,1)}, bf16[4096,4096]{0,1:T(8,128)(2,1)}, u32[]{:S(2)}, u32[]{:S(2)}) %collective-permute-start.3) | collective-permute-done | bytes 33554464 | tf_op jit(solution)/shard_map/ppermute | solution.py:58
  2142.3 115.3 %multiply_multiply_fusion = (f32[4096,6,128]{2,0,1:T(8,128)}, f32[4096,6,128]{2,0,1:T(8,128)}) fusion(f32[6,128]{1,0:T(8,128)S(1)} %get-tuple-element.4, f32[4096,6]{0,1:T(8,128)S(1)} %bitcast.54, bf16[6,128,8192]{2,1,0:T(8,128)(2,1)} %bitcast.51, bf16[4096,4096]{0,1:T(8,128)(2,1)} %collective-permute-done.3, bf16[4096,4096]{0,1:T(8,128)(2,1)} %maximum_select_fusion.1, ...), kind=kOutput, calls=%fused_computation.7 | convolution fusion | flops 51851034624 | bytes 104958976 | tf_op jit(solution)/shard_map/dot_general | solution.py:63
  2257.6 11.3 fusion.20
  2268.9 0.9 collective-permute-start.5
  2269.8 0.1 constant_dynamic-slice_fusion
  2269.9 1.3 collective-permute-done.5
  2271.2 0.8 fusion.9
  (14 shorter events, 0.1 us)
Async XLA Ops:
  0.6 92.7 %collective-permute-start = (bf16[512,4096]{0,1:T(8,128)(2,1)}, bf16[512,4096]{0,1:T(8,128)(2,1)}, u32[]{:S(2)}, u32[]{:S(2)}) collective-permute-start(bf16[512,4096]{0,1:T(8,128)(2,1)} %bitcast.52), channel_id=1, source_target_pairs={{0,2},{2,0},{4,6},{6,4},{8,10},{10,8},{12,14},{14,12},{16,18},{18,... | collective-permute-start | bytes 12582920 | tf_op jit(solution)/shard_map/ppermute | solution.py:58
  104.9 181.0 %collective-permute-start.1 = (bf16[1024,4096]{0,1:T(8,128)(2,1)}, bf16[1024,4096]{0,1:T(8,128)(2,1)}, u32[]{:S(2)}, u32[]{:S(2)}) collective-permute-start(bf16[1024,4096]{0,1:T(8,128)(2,1)} %maximum_select_fusion.3), channel_id=1, source_target_pairs={{0,4},{2,6},{4,0},{6,2},{8,12},{10,14},{12,8},{14,10},{16,20},{18,... | collective-permute-start | bytes 25165832 | tf_op jit(solution)/shard_map/ppermute | solution.py:58
  306.6 359.9 %collective-permute-start.2 = (bf16[2048,4096]{0,1:T(8,128)(2,1)}, bf16[2048,4096]{0,1:T(8,128)(2,1)}, u32[]{:S(2)}, u32[]{:S(2)}) collective-permute-start(bf16[2048,4096]{0,1:T(8,128)(2,1)} %maximum_select_fusion.2), channel_id=1, source_target_pairs={{0,8},{2,10},{4,12},{6,14},{8,0},{10,2},{12,4},{14,6},{16,24},{18,... | collective-permute-start | bytes 50331656 | tf_op jit(solution)/shard_map/ppermute | solution.py:58
  307.5 394.8 %copy-start = (bf16[6,2048,128]{2,1,0:T(8,128)(2,1)S(1)}, bf16[6,2048,128]{2,1,0:T(8,128)(2,1)}, u32[]{:S(2)}) copy-start(bf16[6,2048,128]{2,1,0:T(8,128)(2,1)} %param.8) | copy-start | bytes 9437188
  307.5 398.5 %copy-start.2 = (s32[6,32]{1,0:T(8,128)S(1)}, s32[6,32]{1,0:T(8,128)}, u32[]{:S(2)}) copy-start(s32[6,32]{1,0:T(8,128)} %param.10) | copy-start | bytes 2308
  307.5 398.5 %copy-start.3 = (s32[64]{0:T(128)S(1)}, s32[64]{0:T(128)}, u32[]{:S(2)}) copy-start(s32[64]{0:T(128)} %param.13) | copy-start | bytes 772
  307.5 398.8 %copy-start.5 = (s32[6]{0:T(128)S(1)}, s32[6]{0:T(128)}, u32[]{:S(2)}) copy-start(s32[6]{0:T(128)} %param.11) | copy-start | bytes 76
  307.5 399.2 %copy-start.4 = (s32[6]{0:T(128)S(1)}, s32[6]{0:T(128)}, u32[]{:S(2)}) copy-start(s32[6]{0:T(128)} %param.12) | copy-start | bytes 76
  700.7 1441.6 %collective-permute-start.3 = (bf16[4096,4096]{0,1:T(8,128)(2,1)}, bf16[4096,4096]{0,1:T(8,128)(2,1)}, u32[]{:S(2)}, u32[]{:S(2)}) collective-permute-start(bf16[4096,4096]{0,1:T(8,128)(2,1)} %maximum_select_fusion.1), channel_id=1, source_target_pairs={{0,16},{2,18},{4,20},{6,22},{8,24},{10,26},{12,28},{14,30},{16,0},... | collective-permute-start | bytes 100663304 | tf_op jit(solution)/shard_map/ppermute | solution.py:58
  702.3 9.1 collective-permute-start.4
  2257.6 13.6 copy-start.1
  2268.9 2.3 collective-permute-start.5
